TPU v7x, 512 devices: a whole 4x8x8 slice. The times are simulated.
512 devices in a mesh: freq: 8 (over x, core), geo: 64 (over z, y).
Axes of the slice: x: 4, y: 8, z: 8, core: 2. Of those that a mesh axis runs over, the one named last changes fastest.
Arguments:
- energy: float32 [256, 48, 36, 128], P('geo', 'freq'), may hold values from 0.1 to 1.5
- water_depth: float32 [256, 128], P('geo'), may hold values from 0.5 to 4
- wet_mask: int32 [256, 128], P('geo'), may hold values 0 or 1
- vegetation: int32 [256, 128], P('geo'), may hold values 0 or 1
- canopy: float32 [256, 128], P('geo'), may hold values from 0.004 to 0.04
- quad_offsets: int32 [4], replicated, may hold values from 1 to 3, as said below
- quad_weights: float32 [2], replicated, may hold values from 0.2 to 0.8
Outputs:
- energy_next: float32 [256, 48, 36, 128], P('geo', 'freq')
- orbital: float32 [256, 128], P('geo')
Inputs may be any that keep to these rules, and one draw needn't show every extreme that they name: `quad_offsets`: offsets a and the two direction turns lie in 1 .. 3; the lower frequency offset b equals 3 in every draw.
All inputs are finite; a program needn't handle non-finite values. No bound on the sum of `wet_mask` or of `vegetation` on one device may be relied on, other than what follows from the above.
Results may differ from a plain program's by a relative error of at most 0.00002.
Values sent between devices are 32-bit elements; how exact they have to be, the bound alone decides.
No kernel may reach another device: no remote copies, remote signals or barrier semaphores. Data moves between devices by JAX's collectives and lax.ppermute only.
A program may use at most 64 MiB of HBM per device.

v0:
```python
import math
import jax
import jax.numpy as jnp
from jax import lax
from jax.sharding import PartitionSpec as P

FH = 4
SUBSTEPS = 8
gravity = 9.81
base_freq = 0.03
freq_ratio = 1.05
cell_size = 20.0
sub_step = 2.0
coupling = 0.01
coef_plus = 0.4096
coef_minus = 3.1605
coef_both = 2.589


def from_neighbour(block, axis, distance, cyclic=False):
    count = lax.axis_size(axis)
    if cyclic:
        pairs = [(i, (i + distance) % count) for i in range(count)]
    else:
        pairs = [(i, i + distance) for i in range(count) if 0 <= i + distance < count]
    return lax.ppermute(block, axis, pairs)


def halo(block, axis, dim, width, side, cyclic=False):
    size = block.shape[dim]
    parts = []
    distance = 1
    need = width
    while need > 0:
        take = min(size, need)
        if side < 0:
            piece = lax.slice_in_dim(block, size - take, size, axis=dim)
            parts.insert(0, from_neighbour(piece, axis, distance, cyclic))
        else:
            piece = lax.slice_in_dim(block, 0, take, axis=dim)
            parts.append(from_neighbour(piece, axis, -distance, cyclic))
        need -= take
        distance += 1
    return parts


def butterfly_sum(value, axis):
    count = lax.axis_size(axis)
    assert count & count - 1 == 0
    step = 1
    while step < count:
        value = value + lax.ppermute(value, axis, [(i, i ^ step) for i in range(count)])
        step *= 2
    return value


def gathered_sum(known, index, count, value):
    reach = max(known)
    if count > 2 * (2 * reach + 1) - 2 or count % 2:
        return butterfly_sum(value, "freq")
    far = count // 2
    ordered = jnp.stack([known[o] for o in range(-reach, reach + 1)])
    more = from_neighbour(ordered, "freq", far, True)
    table = []
    for rel in range(count):
        off = rel if rel <= reach else rel - count
        if -reach <= off <= reach:
            table.append(known[off])
        else:
            table.append(more[rel - far + reach])
    table = jnp.stack(table)
    table = jnp.concatenate([table, table], axis=0)
    start = (count - index) % count
    glob = lax.dynamic_slice_in_dim(table, start, count, axis=0)
    while glob.shape[0] > 1:
        glob = glob[0::2] + glob[1::2]
    return glob[0]


def physics(radian_freq, water_depth, dir_count):
    square = (radian_freq * radian_freq)[None, :, None]
    column = water_depth[:, None, :]
    depth_ratio = square * column / gravity
    depth_wave = depth_ratio / jnp.sqrt(jnp.tanh(depth_ratio))
    group_speed = (
        radian_freq[None, :, None]
        * column
        / depth_wave
        * (0.5 + depth_wave / jnp.sinh(2.0 * depth_wave))
    )
    orbit_weight = (
        square
        / jnp.sinh(depth_wave) ** 2
        * (radian_freq * (freq_ratio - 1.0))[None, :, None]
        * (2.0 * math.pi / dir_count)
    )
    return (group_speed, orbit_weight)


def angles_of(dir_count):
    angles = (jnp.arange(dir_count, dtype=jnp.float32) + 0.5) * (2.0 * math.pi / dir_count)
    return (jnp.cos(angles), jnp.sin(angles))


def shifted(doubled, freq_start, dir_off, count):
    dir_count = doubled.shape[2] // 2
    starts = (jnp.zeros((), jnp.int32), freq_start, dir_off % dir_count, jnp.zeros((), jnp.int32))
    return lax.dynamic_slice(
        doubled, starts, (doubled.shape[0], count, dir_count, doubled.shape[3])
    )


def source_change(extended, quad_offsets, quad_weights, count):
    up_bins, down_bins, up_turn, down_turn = (
        quad_offsets[0],
        quad_offsets[1],
        quad_offsets[2],
        quad_offsets[3],
    )
    weight_up, weight_down = (quad_weights[0], quad_weights[1])
    wide = count + 2 * FH
    doubled = jnp.concatenate([extended, extended], axis=2)
    centre = lax.slice_in_dim(extended, FH, FH + wide, axis=1)
    upper = weight_up * shifted(doubled, FH + up_bins, up_turn, wide) + (1.0 - weight_up) * shifted(
        doubled, FH + up_bins + 1, up_turn, wide
    )
    lower = weight_down * shifted(doubled, FH - down_bins, -down_turn, wide) + (
        1.0 - weight_down
    ) * shifted(doubled, FH - down_bins - 1, -down_turn, wide)
    transfer = coupling * (
        centre * centre * (coef_plus * upper + coef_minus * lower)
        - coef_both * centre * upper * lower
    )
    spread = jnp.concatenate([transfer, transfer], axis=2)
    gained = weight_up * shifted(spread, FH - up_bins, -up_turn, count) + (
        1.0 - weight_up
    ) * shifted(spread, FH - up_bins - 1, -up_turn, count)
    gained = (
        gained
        + weight_down * shifted(spread, FH + down_bins, down_turn, count)
        + (1.0 - weight_down) * shifted(spread, FH + down_bins + 1, down_turn, count)
    )
    own = lax.slice_in_dim(transfer, FH, FH + count, axis=1)
    return gained - 2.0 * own


def east_west(east_flux, cosines):
    zeros = jnp.zeros_like(east_flux[..., :1])
    behind = jnp.concatenate([zeros, east_flux[..., :-1]], axis=-1)
    ahead = jnp.concatenate([east_flux[..., 1:], zeros], axis=-1)
    east_going = (cosines > 0.0)[None, None, :, None]
    return jnp.where(east_going, east_flux - behind, ahead - east_flux)


def propagate(spectrum, speed, wet, cosines, sines, northward):
    step_ratio = sub_step / cell_size
    east_speed = speed[:, :, None, :] * cosines[None, None, :, None]
    north_speed = speed[:, :, None, :] * sines[None, None, :, None]
    rows = spectrum.shape[0]
    for substep in range(SUBSTEPS):
        lo, hi = (substep, rows) if northward else (0, rows - substep)
        east_flux = east_speed[lo:hi] * spectrum
        north_flux = north_speed[lo:hi] * spectrum
        along = north_flux[1:] - north_flux[:-1]
        across = east_west(east_flux, cosines)
        if northward:
            spectrum = wet[lo + 1 : hi, None, None, :] * (
                spectrum[1:] - step_ratio * (across[1:] + along)
            )
        else:
            spectrum = wet[lo : hi - 1, None, None, :] * (
                spectrum[:-1] - step_ratio * (across[:-1] + along)
            )
    return spectrum


def body(energy, water_depth, wet_mask, vegetation, canopy, quad_offsets, quad_weights):
    tile_rows, freq_count, dir_count, tile_cols = energy.shape
    wet_field = wet_mask.astype(jnp.float32)
    veg_field = vegetation.astype(jnp.float32)
    wet_four = wet_field[:, None, None, :]
    masked = wet_four * energy
    first_bin = lax.axis_index("freq") * freq_count
    bin_index = (first_bin + jnp.arange(freq_count, dtype=jnp.int32)).astype(jnp.float32)
    radian_freq = 2.0 * math.pi * base_freq * jnp.power(freq_ratio, bin_index)
    half = dir_count // 2
    cosines, sines = angles_of(dir_count)
    fields = jnp.zeros((tile_rows, 1, half, tile_cols), jnp.float32)
    fields = fields.at[:, 0, 0, :].set(wet_field).at[:, 0, 1, :].set(water_depth)
    north_msg = jnp.concatenate([masked[:, :, :half], fields], axis=1)
    south_msg = jnp.concatenate([masked[:, :, half:], fields], axis=1)
    below = halo(north_msg, "geo", 0, SUBSTEPS, -1)
    above = halo(south_msg, "geo", 0, SUBSTEPS, +1)
    group_speed, orbit_weight = physics(radian_freq, water_depth, dir_count)
    partial_value = jnp.sum(orbit_weight * jnp.sum(energy, axis=2), axis=1)
    freq_index = lax.axis_index("freq")
    freq_total = lax.axis_size("freq")
    slot = jnp.zeros((tile_rows, 1, dir_count, tile_cols), jnp.float32)
    slot = slot.at[:, 0, 0, :].set(partial_value)
    gathered = lax.all_gather(jnp.concatenate([masked, slot], axis=1), "freq", axis=1, tiled=True)
    gathered = gathered.reshape(tile_rows, freq_total, freq_count + 1, dir_count, tile_cols)
    partials = gathered[:, :, freq_count, 0, :]
    spectrum_all = gathered[:, :, :freq_count].reshape(
        tile_rows, freq_total * freq_count, dir_count, tile_cols
    )
    padded_all = jnp.pad(spectrum_all, ((0, 0), (2 * FH, 2 * FH), (0, 0), (0, 0)))
    extended = lax.dynamic_slice_in_dim(padded_all, first_bin, freq_count + 4 * FH, axis=1)
    glob = jnp.moveaxis(partials, 1, 0)
    while glob.shape[0] > 1:
        glob = glob[0::2] + glob[1::2]
    orbital = jnp.sqrt(glob[0])
    full_step = SUBSTEPS * sub_step
    damping = 1.0 + full_step * canopy * veg_field * orbital
    change = source_change(extended, quad_offsets, quad_weights, freq_count)
    increment = (masked + full_step * change) / damping[:, None, None, :] - masked
    geo_index = lax.axis_index("geo")
    geo_count = lax.axis_size("geo")

    def unpack(parts, offsets):
        spectra, speeds, wets = ([], [], [])
        for part, offset in zip(parts, offsets):
            valid = (geo_index + offset >= 0) & (geo_index + offset < geo_count)
            depth = jnp.where(valid, part[:, freq_count, 1, :], 1.0)
            spectra.append(part[:, :freq_count])
            wets.append(part[:, freq_count, 0, :])
            speeds.append(physics(radian_freq, depth, dir_count)[0])
        return (spectra, speeds, wets)

    n_off = [-(len(below) - k) for k in range(len(below))]
    b_spec, b_speed, b_wet = unpack(below, n_off)
    north = propagate(
        jnp.concatenate(b_spec + [masked[:, :, :half]], axis=0),
        jnp.concatenate(b_speed + [group_speed], axis=0),
        jnp.concatenate(b_wet + [wet_field], axis=0),
        cosines[:half],
        sines[:half],
        True,
    )
    s_off = [k + 1 for k in range(len(above))]
    a_spec, a_speed, a_wet = unpack(above, s_off)
    south = propagate(
        jnp.concatenate([masked[:, :, half:]] + a_spec, axis=0),
        jnp.concatenate([group_speed] + a_speed, axis=0),
        jnp.concatenate([wet_field] + a_wet, axis=0),
        cosines[half:],
        sines[half:],
        False,
    )
    moved = jnp.concatenate([north, south], axis=2)
    return (wet_four * (moved + increment), orbital)


def solution(mesh):
    placed = (
        P("geo", "freq", None, None),
        P("geo", None),
        P("geo", None),
        P("geo", None),
        P("geo", None),
        P(),
        P(),
    )
    return jax.shard_map(
        body,
        mesh=mesh,
        in_specs=placed,
        out_specs=(P("geo", "freq", None, None), P("geo", None)),
        check_vma=False,
    )
```

profile of v0, /device:TPU:1, one launch (start us, length us, event | category | flops | bytes accessed | tf_op | source)
XLA Modules:
  0.0 115.2 jit_solution(11909362313528127280)
XLA Ops:
  7.2 0.7 fusion.169
  7.9 1.1 fusion.159
  9.1 0.6 slice.640
  9.7 1.3 %constant_dynamic-update-slice_fusion = f32[4,1,18,128]{3,0,2,1:T(4,128)S(1)} fusion(f32[4,1,18,128]{3,0,2,1:T(4,128)S(1)} %scatter.10, s32[]{:T(128)} %bitcast.2, f32[4,128]{1,0:T(4,128)} %param.14), kind=kLoop, calls=%fused_computation.258 | loop fusion | bytes 4100 | tf_op jit(solution)/shard_map/scatter | solution.py:189
  11.1 1.3 %collective-permute-start.2 = (f32[4,7,18,128]{3,0,2,1:T(4,128)S(1)}, f32[4,7,18,128]{3,0,2,1:T(4,128)S(1)}, u32[]{:S(2)}, u32[]{:S(2)}) collective-permute-start(f32[4,7,18,128]{3,0,2,1:T(4,128)S(1)} %get-tuple-element.123), channel_id=1, source_target_pairs={{1,0},{2,1},{3,2},{4,3},{5,4},{6,5},{7,6},{8,7},{9,8},{10,9},{11,1... | collective-permute-start | bytes 774152 | tf_op jit(solution)/shard_map/ppermute | solution.py:26
  12.4 1.3 %collective-permute-start.3 = (f32[4,7,18,128]{3,0,2,1:T(4,128)S(1)}, f32[4,7,18,128]{3,0,2,1:T(4,128)S(1)}, u32[]{:S(2)}, u32[]{:S(2)}) collective-permute-start(f32[4,7,18,128]{3,0,2,1:T(4,128)S(1)} %get-tuple-element.123), channel_id=1, source_target_pairs={{2,0},{3,1},{4,2},{5,3},{6,4},{7,5},{8,6},{9,7},{10,8},{11,9},{12,... | collective-permute-start | bytes 774152 | tf_op jit(solution)/shard_map/ppermute | solution.py:26
  13.7 6.5 %collective-permute-start.1 = (f32[4,7,18,128]{3,0,2,1:T(4,128)S(1)}, f32[4,7,18,128]{3,0,2,1:T(4,128)S(1)}, u32[]{:S(2)}, u32[]{:S(2)}) collective-permute-start(f32[4,7,18,128]{3,0,2,1:T(4,128)S(1)} %get-tuple-element.122), channel_id=1, source_target_pairs={{0,2},{1,3},{2,4},{3,5},{4,6},{5,7},{6,8},{7,9},{8,10},{9,11},{10,... | collective-permute-start | bytes 774152 | tf_op jit(solution)/shard_map/ppermute | solution.py:26
  20.2 3.2 %collective-permute-start = (f32[4,7,18,128]{3,0,2,1:T(4,128)S(1)}, f32[4,7,18,128]{3,0,2,1:T(4,128)S(1)}, u32[]{:S(2)}, u32[]{:S(2)}) collective-permute-start(f32[4,7,18,128]{3,0,2,1:T(4,128)S(1)} %get-tuple-element.122), channel_id=1, source_target_pairs={{0,1},{1,2},{2,3},{3,4},{4,5},{5,6},{6,7},{7,8},{8,9},{9,10},{10,1... | collective-permute-start | bytes 774152 | tf_op jit(solution)/shard_map/ppermute | solution.py:26
  23.6 0.5 fusion.172
  24.1 1.3 %fusion.170 = (f32[1]{0:T(128)}, f32[1]{0:T(128)}) fusion(f32[2]{0:T(128)} %param.19), kind=kLoop, calls=%fused_computation.307 | loop fusion | bytes 16 | tf_op jit(solution)/shard_map/slice | solution.py:120
  25.4 1.5 %fusion.171 = (s32[1]{0:T(128)}, s32[1]{0:T(128)}, s32[1]{0:T(128)}, s32[1]{0:T(128)}) fusion(s32[4]{0:T(128)} %param.18), kind=kLoop, calls=%fused_computation.308 | loop fusion | bytes 32 | tf_op jit(solution)/shard_map/slice | solution.py:117
  40.5 0.6 slice.815
  41.1 0.6 slice.814
  41.7 0.6 slice.813
  42.3 0.6 slice.644
  42.9 0.6 slice.643
  43.5 0.6 slice.642
  44.1 1.0 multiply_reduce_fusion
  45.1 0.6 pad_maximum_fusion.4
  45.8 0.4 fusion.96
  46.2 0.3 fusion.158
  46.6 0.6 slice_multiply_fusion.5
  47.6 0.6 slice_multiply_fusion.3
  48.1 0.3 fusion.156
  48.6 0.6 slice_multiply_fusion.1
  49.6 0.3 slice_multiply_fusion.20
  50.2 0.3 slice_multiply_fusion.18
  51.9 0.9 select_maximum_fusion
  52.8 1.0 slice.817
  53.8 1.2 %fusion.94 = (f32[12,6,18,128]{3,0,2,1:T(8,128)S(1)}, f32[12,6,18,128]{3,0,2,1:T(8,128)S(1)}, f32[12,6,18,128]{3,0,2,1:T(8,128)S(1)}, f32[12,6,18,128]{3,0,2,1:T(8,128)S(1)}, f32[12,6,18,128]{3,0,2,1:T(8,128)S(1)}) fusion(f32[18]{0:T(128)} %get-tuple-element.155, f32[12,6,128]{2,0,1:T(8,128)} %get-tuple-element.124, ...), kind=kLoop, calls=%fused_computation.195 | loop fusion | flops 995328 | bytes 4018320 | tf_op jit(solution)/shard_map/mul | solution.py:162
  55.1 0.3 fusion.154
  55.4 0.8 slice_multiply_fusion.11
  56.8 0.8 slice_multiply_fusion.9
  57.6 0.3 fusion.152
  58.3 0.8 slice_multiply_fusion.7
  59.1 0.3 fusion.151
  59.5 0.5 slice_multiply_fusion.28
  60.3 0.4 slice_multiply_fusion.26
  61.0 0.6 slice_multiply_fusion.24
  61.8 0.4 slice_multiply_fusion.22
  62.5 0.6 fusion.106
  63.2 34.5 %all-gather.2.cloned.1.call-done = f32[4,56,36,128]{3,0,2,1:T(4,128)} async-done(((f32[4,7,36,128]{3,0,2,1:T(4,128)}), f32[4,56,36,128]{3,0,2,1:T(4,128)}) %all-gather.2.cloned.1.call-update) | async-done | bytes 4128784 | tf_op jit(solution)/shard_map/all_gather | solution.py:200
  97.6 2.2 %slice.954 = f32[4,8,6,36,128]{4,0,3,2,1:T(4,128)S(1)} slice(f32[4,8,7,36,128]{4,0,3,2,1:T(4,128)} %bitcast.61), slice={[0:4], [0:8], [0:6], [0:36], [0:128]} | slice | bytes 7077888 | tf_op jit(solution)/shard_map/slice | solution.py:203
  99.9 0.7 slice_bitcast_fusion
  100.6 0.3 pad_dynamic-slice_fusion.1
  101.0 0.6 multiply_add_fusion
  101.6 3.8 %subtract_multiply_fusion = f32[4,14,36,128]{3,0,2,1:T(4,128)S(1)} fusion(s32[]{:T(128)S(6)} %select_n.216, s32[]{:T(128)S(6)} %select_n.215, f32[4,22,36,128]{3,0,2,1:T(4,128)S(1)} %pad_dynamic-slice_fusion.1, s32[]{:T(128)S(6)} %select_n.213, s32[]{:T(128)S(6)} %select_n.212, s32[]{:T(128)S(6)} %select_n.211, s32[]{:T(128)S(6)} %select_n.209, ...), kind=kLoop, calls=%fused_computation.28 | loop fusion | flops 5160960 | bytes 6193196 | tf_op jit(solution)/shard_map/mul | solution.py:130
  105.4 3.0 %fusion.93 = f32[4,6,36,128]{3,0,2,1:T(4,128)} fusion(f32[4,6,18,128]{3,0,2,1:T(4,128)S(1)} %get-tuple-element.129, f32[4,6,18,128]{3,0,2,1:T(4,128)S(1)} %get-tuple-element.128, f32[4,14,36,128]{3,0,2,1:T(4,128)S(1)} %subtract_multiply_fusion, s32[]{:T(128)S(6)} %select_n.224, s32[]{:T(128)S(6)} %select_n.223, s32[]{:T(128)S(6)} %select_n.221, ...), kind=kLoop, calls=%fused_computation.192 | loop fusion | flops 2322432 | bytes 2805800 | tf_op jit(solution)/shard_map/mul | solution.py:250
  (76 shorter events, 5.4 us)
Async XLA Ops:
  7.2 90.5 %all-gather.2.cloned.1.call-start = ((), (), s32[]{:S(2)}) async-start(), calls=%async_computation | async-start | bytes 4644864 | tf_op jit(solution)/shard_map/all_gather | solution.py:200
  11.1 29.2 %collective-permute-start.2 = (f32[4,7,18,128]{3,0,2,1:T(4,128)S(1)}, f32[4,7,18,128]{3,0,2,1:T(4,128)S(1)}, u32[]{:S(2)}, u32[]{:S(2)}) collective-permute-start(f32[4,7,18,128]{3,0,2,1:T(4,128)S(1)} %get-tuple-element.123), channel_id=1, source_target_pairs={{1,0},{2,1},{3,2},{4,3},{5,4},{6,5},{7,6},{8,7},{9,8},{10,9},{11,1... | collective-permute-start | bytes 774152 | tf_op jit(solution)/shard_map/ppermute | solution.py:26
  12.4 28.0 %collective-permute-start.3 = (f32[4,7,18,128]{3,0,2,1:T(4,128)S(1)}, f32[4,7,18,128]{3,0,2,1:T(4,128)S(1)}, u32[]{:S(2)}, u32[]{:S(2)}) collective-permute-start(f32[4,7,18,128]{3,0,2,1:T(4,128)S(1)} %get-tuple-element.123), channel_id=1, source_target_pairs={{2,0},{3,1},{4,2},{5,3},{6,4},{7,5},{8,6},{9,7},{10,8},{11,9},{12,... | collective-permute-start | bytes 774152 | tf_op jit(solution)/shard_map/ppermute | solution.py:26
  13.7 26.7 %collective-permute-start.1 = (f32[4,7,18,128]{3,0,2,1:T(4,128)S(1)}, f32[4,7,18,128]{3,0,2,1:T(4,128)S(1)}, u32[]{:S(2)}, u32[]{:S(2)}) collective-permute-start(f32[4,7,18,128]{3,0,2,1:T(4,128)S(1)} %get-tuple-element.122), channel_id=1, source_target_pairs={{0,2},{1,3},{2,4},{3,5},{4,6},{5,7},{6,8},{7,9},{8,10},{9,11},{10,... | collective-permute-start | bytes 774152 | tf_op jit(solution)/shard_map/ppermute | solution.py:26
  20.2 20.2 %collective-permute-start = (f32[4,7,18,128]{3,0,2,1:T(4,128)S(1)}, f32[4,7,18,128]{3,0,2,1:T(4,128)S(1)}, u32[]{:S(2)}, u32[]{:S(2)}) collective-permute-start(f32[4,7,18,128]{3,0,2,1:T(4,128)S(1)} %get-tuple-element.122), channel_id=1, source_target_pairs={{0,1},{1,2},{2,3},{3,4},{4,5},{5,6},{6,7},{7,8},{8,9},{9,10},{10,1... | collective-permute-start | bytes 774152 | tf_op jit(solution)/shard_map/ppermute | solution.py:26
  40.4 5.4 %copy-start.2 = (f32[4,7,18,128]{3,0,2,1:T(4,128)}, f32[4,7,18,128]{3,0,2,1:T(4,128)S(1)}, u32[]{:S(2)}) copy-start(f32[4,7,18,128]{3,0,2,1:T(4,128)S(1)} %collective-permute-done) | copy-start | bytes 774148
  40.4 6.1 %copy-start.1 = (f32[4,7,18,128]{3,0,2,1:T(4,128)}, f32[4,7,18,128]{3,0,2,1:T(4,128)S(1)}, u32[]{:S(2)}) copy-start(f32[4,7,18,128]{3,0,2,1:T(4,128)S(1)} %collective-permute-done.1) | copy-start | bytes 774148
  51.7 2.1 %slice-start = ((f32[4,7,18,128]{3,0,2,1:T(4,128)}), f32[4,6,18,128]{3,0,2,1:T(4,128)S(1)}, s32[]{:S(2)}) async-start(f32[4,7,18,128]{3,0,2,1:T(4,128)} %copy-done.1), calls=%async_computation.1 | async-start | bytes 442368 | tf_op jit(solution)/shard_map/slice | solution.py:224
  53.8 1.6 %copy-start.5 = (f32[11,128]{1,0:T(8,128)S(1)}, f32[11,128]{1,0:T(8,128)}, u32[]{:S(2)}) copy-start(f32[11,128]{1,0:T(8,128)} %slice.815) | copy-start | bytes 16900
  56.1 0.7 copy-start.4
  57.6 0.7 copy-start.3
  59.5 0.8 copy-start.8
  60.3 0.7 copy-start.7
  61.0 0.9 copy-start.6
  99.9 1.1 copy-start.9
  99.9 1.1 copy-start.10
  101.0 4.4 %copy-start = (f32[4,6,36,128]{3,0,2,1:T(4,128)S(1)}, f32[4,6,36,128]{3,0,2,1:T(4,128)}, u32[]{:S(2)}) copy-start(f32[4,6,36,128]{3,0,2,1:T(4,128)} %param.13) | copy-start | bytes 1327108
Sparse Core Ops, SparseCore 0:
  52.9 44.6 all-gather.1
where the time goes:
time: 116 us; the launch traced here: 115 us
  waiting for transfers between devices  34.5 us (30%)
  between operations  28 us (24%)
  other arithmetic  22.8 us (20%)
  local copies, waits for them, and re-layouts  17.7 us (15%)
  starting transfers between devices  12.3 us (11%)
    all_gather x1, waiting for transfers between devices, body(): lax.all_gather(jnp.concatenate([masked, slot], axis=1), 'freq', axis=1, t...  34.5 us
    ppermute x4, starting transfers between devices, from_neighbour(): return lax.ppermute(block, axis, pairs)  12.3 us
    mul x16, other arithmetic, propagate(): east_flux = east_speed[lo:hi] * spectrum  8.76 us
    slice x16, local copies, waits for them, and re-layouts, east_west(): behind = jnp.concatenate([zeros, east_flux[..., :-1]], axis=-1)  3.96 us
    mul x1, other arithmetic, source_change(): coupling * (centre * centre * (coef_plus * upper + coef_minus * lower) -...  3.76 us
    slice x6, local copies, waits for them, and re-layouts, propagate(): wet[lo + 1:hi, None, None, :]  3.61 us
    mul x1, other arithmetic, body(): return (wet_four * (moved + increment), orbital)  3.01 us
  transfers between devices with their start and end apart: 5, of which 1 were waited for; matrix products, arithmetic and copies ran while one was open for 11% of the time, Pallas kernels for 0%

commit v1 on v0

--- a/solution.py
+++ b/solution.py
@@ -197,7 +197,15 @@
     freq_total = lax.axis_size("freq")
     slot = jnp.zeros((tile_rows, 1, dir_count, tile_cols), jnp.float32)
     slot = slot.at[:, 0, 0, :].set(partial_value)
-    gathered = lax.all_gather(jnp.concatenate([masked, slot], axis=1), "freq", axis=1, tiled=True)
+    gathered = jnp.concatenate(
+        lax.all_to_all(
+            jnp.stack([jnp.concatenate([masked, slot], axis=1)] * lax.axis_size("freq")),
+            "freq",
+            0,
+            0,
+        ),
+        axis=1,
+    )
     gathered = gathered.reshape(tile_rows, freq_total, freq_count + 1, dir_count, tile_cols)
     partials = gathered[:, :, freq_count, 0, :]
     spectrum_all = gathered[:, :, :freq_count].reshape(

time: 116 us -> 124 us (1.069)
  between operations: 28 us -> 15.2 us
  starting transfers between devices: 12.3 us -> 23.9 us
  waiting for transfers between devices: 34.5 us -> 41 us
  other arithmetic: 22.8 us -> 25.2 us
    all_to_all x0 -> x1, waiting for transfers between devices: none -> 41 us  [body(): lax.all_to_all(jnp.stack([jnp.concatenate([masked, slot], axis=1)] * lax....]
    all_gather x1 -> x0, waiting for transfers between devices: 34.5 us -> none  [body(): lax.all_gather(jnp.concatenate([masked, slot], axis=1), 'freq', axis=1, t...]
    all_to_all x0 -> x1, starting transfers between devices: none -> 11.6 us  [body(): lax.all_to_all(jnp.stack([jnp.concatenate([masked, slot], axis=1)] * lax....]
    slice x6, local copies, waits for them, and re-layouts: 3.61 us -> 0.03 us  [propagate(): wet[lo + 1:hi, None, None, :]]
    another operation x2 -> x3, local copies, waits for them, and re-layouts: 0.58 us -> 3.11 us  [the longest x1 2.53 us: body(): jnp.stack([jnp.concatenate([masked, slot], axis=1)] * lax.axis_size('freq'))]
    slice x16, local copies, waits for them, and re-layouts: 3.96 us -> 6.08 us  [east_west(): behind = jnp.concatenate([zeros, east_flux[..., :-1]], axis=-1)]
    mul x14, other arithmetic: 1.34 us -> 3.3 us  [propagate(): north_flux = north_speed[lo:hi] * spectrum]
    mul x16, other arithmetic: 8.76 us -> 10.4 us  [propagate(): east_flux = east_speed[lo:hi] * spectrum]
  transfers between devices with their start and end apart: 5 -> 5, of which waited for: 1 -> 1; matrix products, arithmetic and copies ran while one was open for 11% -> 8% of each run, Pallas kernels for 0% -> 0%
where the time goes in v1:
time: 124 us
  waiting for transfers between devices  41 us (33%)
  other arithmetic  25.2 us (20%)
  starting transfers between devices  23.9 us (19%)
  local copies, waits for them, and re-layouts  18.3 us (15%)
  between operations  15.2 us (12%)
    all_to_all x1, waiting for transfers between devices, body(): lax.all_to_all(jnp.stack([jnp.concatenate([masked, slot], axis=1)] * lax....  41 us
    ppermute x4, starting transfers between devices, from_neighbour(): return lax.ppermute(block, axis, pairs)  12.3 us
    all_to_all x1, starting transfers between devices, body(): lax.all_to_all(jnp.stack([jnp.concatenate([masked, slot], axis=1)] * lax....  11.6 us
    mul x16, other arithmetic, propagate(): east_flux = east_speed[lo:hi] * spectrum  10.4 us
    slice x16, local copies, waits for them, and re-layouts, east_west(): behind = jnp.concatenate([zeros, east_flux[..., :-1]], axis=-1)  6.08 us
    mul x1, other arithmetic, source_change(): coupling * (centre * centre * (coef_plus * upper + coef_minus * lower) -...  3.88 us
    mul x14, other arithmetic, propagate(): north_flux = north_speed[lo:hi] * spectrum  3.3 us
    mul x1, other arithmetic, body(): return (wet_four * (moved + increment), orbital)  3.13 us
  transfers between devices with their start and end apart: 5, of which 1 were waited for; matrix products, arithmetic and copies ran while one was open for 8% of the time, Pallas kernels for 0%

profile of v1, /device:TPU:1, one launch (start us, length us, event | category | flops | bytes accessed | tf_op | source)
XLA Modules:
  0.0 123.6 jit_solution(9223742887352788762)
XLA Ops:
  0.6 0.7 fusion.169
  1.3 1.1 fusion.159
  2.4 0.8 copy-done.3
  3.2 0.6 slice.640
  3.8 1.3 %constant_dynamic-update-slice_fusion = f32[4,1,18,128]{3,0,2,1:T(4,128)S(1)} fusion(f32[4,1,18,128]{3,0,2,1:T(4,128)S(1)} %scatter.10, s32[]{:T(128)} %bitcast.2, f32[4,128]{1,0:T(4,128)} %param.14), kind=kLoop, calls=%fused_computation.258 | loop fusion | bytes 4100 | tf_op jit(solution)/shard_map/scatter | solution.py:189
  5.3 1.3 %collective-permute-start.2 = (f32[4,7,18,128]{3,0,2,1:T(4,128)S(1)}, f32[4,7,18,128]{3,0,2,1:T(4,128)S(1)}, u32[]{:S(2)}, u32[]{:S(2)}) collective-permute-start(f32[4,7,18,128]{3,0,2,1:T(4,128)S(1)} %get-tuple-element.123), channel_id=1, source_target_pairs={{1,0},{2,1},{3,2},{4,3},{5,4},{6,5},{7,6},{8,7},{9,8},{10,9},{11,1... | collective-permute-start | bytes 774152 | tf_op jit(solution)/shard_map/ppermute | solution.py:26
  6.6 1.3 %collective-permute-start.3 = (f32[4,7,18,128]{3,0,2,1:T(4,128)S(1)}, f32[4,7,18,128]{3,0,2,1:T(4,128)S(1)}, u32[]{:S(2)}, u32[]{:S(2)}) collective-permute-start(f32[4,7,18,128]{3,0,2,1:T(4,128)S(1)} %get-tuple-element.123), channel_id=1, source_target_pairs={{2,0},{3,1},{4,2},{5,3},{6,4},{7,5},{8,6},{9,7},{10,8},{11,9},{12,... | collective-permute-start | bytes 774152 | tf_op jit(solution)/shard_map/ppermute | solution.py:26
  7.9 6.5 %collective-permute-start.1 = (f32[4,7,18,128]{3,0,2,1:T(4,128)S(1)}, f32[4,7,18,128]{3,0,2,1:T(4,128)S(1)}, u32[]{:S(2)}, u32[]{:S(2)}) collective-permute-start(f32[4,7,18,128]{3,0,2,1:T(4,128)S(1)} %get-tuple-element.122), channel_id=1, source_target_pairs={{0,2},{1,3},{2,4},{3,5},{4,6},{5,7},{6,8},{7,9},{8,10},{9,11},{10,... | collective-permute-start | bytes 774152 | tf_op jit(solution)/shard_map/ppermute | solution.py:26
  14.4 3.2 %collective-permute-start = (f32[4,7,18,128]{3,0,2,1:T(4,128)S(1)}, f32[4,7,18,128]{3,0,2,1:T(4,128)S(1)}, u32[]{:S(2)}, u32[]{:S(2)}) collective-permute-start(f32[4,7,18,128]{3,0,2,1:T(4,128)S(1)} %get-tuple-element.122), channel_id=1, source_target_pairs={{0,1},{1,2},{2,3},{3,4},{4,5},{5,6},{6,7},{7,8},{8,9},{9,10},{10,1... | collective-permute-start | bytes 774152 | tf_op jit(solution)/shard_map/ppermute | solution.py:26
  17.9 1.4 %fusion.170 = (f32[1]{0:T(128)}, f32[1]{0:T(128)}) fusion(f32[2]{0:T(128)} %param.19), kind=kLoop, calls=%fused_computation.307 | loop fusion | bytes 16 | tf_op jit(solution)/shard_map/slice | solution.py:120
  19.2 1.4 %fusion.171 = (s32[1]{0:T(128)}, s32[1]{0:T(128)}, s32[1]{0:T(128)}, s32[1]{0:T(128)}) fusion(s32[4]{0:T(128)} %param.18), kind=kLoop, calls=%fused_computation.308 | loop fusion | bytes 32 | tf_op jit(solution)/shard_map/slice | solution.py:117
  34.9 1.0 multiply_reduce_fusion
  35.9 0.4 fusion.96
  36.4 0.3 fusion.158
  36.7 0.6 slice_multiply_fusion.5
  37.2 0.3 fusion.157
  37.7 0.6 slice_multiply_fusion.3
  38.2 0.3 fusion.156
  38.7 0.6 slice_multiply_fusion.1
  39.2 0.3 fusion.155
  39.7 0.3 slice_multiply_fusion.20
  40.3 0.3 slice_multiply_fusion.18
  41.4 1.0 slice_multiply_fusion.14
  42.5 1.1 fusion.165
  43.6 0.4 fusion.94
  44.1 0.3 fusion.154
  44.4 0.7 slice_multiply_fusion.11
  45.1 0.3 fusion.153
  45.5 0.7 slice_multiply_fusion.9
  46.3 0.3 fusion.152
  46.7 0.7 slice_multiply_fusion.7
  47.5 1.5 %fusion.151 = (f32[9,6,18,127]{3,0,2,1:T(8,128)}, f32[9,6,18,127]{3,0,2,1:T(8,128)}) fusion(f32[9,6,18,128]{3,0,2,1:T(8,128)S(1)} %get-tuple-element.48), kind=kLoop, calls=%fused_computation.288 | loop fusion | bytes 1975104 | tf_op jit(solution)/shard_map/slice | solution.py:149
  49.0 1.1 slice_multiply_fusion.6
  50.2 2.5 %stack.2 = f32[8,4,7,36,128]{4,1,3,2,0:T(4,128)} broadcast(f32[4,7,36,128]{3,0,2,1:T(4,128)S(1)} %select_maximum_fusion), dimensions={1,2,3,4} | broadcast | bytes 4644864 | tf_op jit(solution)/shard_map/stack | solution.py:202
  52.7 11.6 %all-to-all-start = ((f32[8,4,7,36,128]{4,1,3,2,0:T(4,128)}), f32[8,4,7,36,128]{4,1,3,2,0:T(4,128)}, u32[]{:S(2)}, u32[]{:S(2)}) async-start(f32[8,4,7,36,128]{4,1,3,2,0:T(4,128)} %stack.2), calls=%async_computation | async-start | bytes 8257536 | tf_op jit(solution)/shard_map/all_to_all | solution.py:201
  64.3 1.1 slice_multiply_fusion.13
  65.4 2.5 %slice_multiply_fusion.28 = (f32[8,6,18,128]{3,0,2,1:T(8,128)S(1)}, f32[8,6,18,128]{3,0,2,1:T(8,128)S(1)}) fusion(f32[12,6,18,128]{3,0,2,1:T(8,128)S(1)} %get-tuple-element.121, f32[9,6,18,128]{3,0,2,1:T(8,128)} %slice_multiply_fusion.6, f32[9,6,18,127]{3,0,2,1:T(8,128)} %get-tuple-element.69, f32[9,6,18,127]{3,0,2,1:T(8,128)} %get-tuple-element.68, ...), kind=kLoop, calls=%fused_computation.179 | loop fusion | flops 995328 | bytes 4088242 | tf_op jit(solution)/shard_map/mul | solution.py:162
  68.3 0.4 slice_multiply_fusion.26
  68.9 0.4 slice_multiply_fusion.24
  69.7 0.4 slice_multiply_fusion.22
  71.0 0.5 fusion.106
  71.6 41.0 %all-to-all-done = f32[8,4,7,36,128]{4,1,3,2,0:T(4,128)} async-done(((f32[8,4,7,36,128]{4,1,3,2,0:T(4,128)}), f32[8,4,7,36,128]{4,1,3,2,0:T(4,128)}, u32[]{:S(2)}, u32[]{:S(2)}) %all-to-all-start) | async-done | bytes 4128800 | tf_op jit(solution)/shard_map/all_to_all | solution.py:201
  112.6 2.2 %slice.954 = f32[4,8,6,36,128]{4,0,3,2,1:T(4,128)S(1)} slice(f32[4,8,7,36,128]{4,0,3,2,1:T(4,128)} %bitcast.13), slice={[0:4], [0:8], [0:6], [0:36], [0:128]} | slice | bytes 7077888 | tf_op jit(solution)/shard_map/slice | solution.py:211
  114.8 0.7 slice_bitcast_fusion
  115.5 0.3 pad_dynamic-slice_fusion.1
  115.9 0.6 multiply_add_fusion
  116.5 3.9 %subtract_multiply_fusion = f32[4,14,36,128]{3,0,2,1:T(4,128)S(1)} fusion(s32[]{:T(128)S(6)} %select_n.216, s32[]{:T(128)S(6)} %select_n.215, f32[4,22,36,128]{3,0,2,1:T(4,128)S(1)} %pad_dynamic-slice_fusion.1, s32[]{:T(128)S(6)} %select_n.213, s32[]{:T(128)S(6)} %select_n.212, s32[]{:T(128)S(6)} %select_n.211, s32[]{:T(128)S(6)} %select_n.209, ...), kind=kLoop, calls=%fused_computation.28 | loop fusion | flops 5160960 | bytes 6193196 | tf_op jit(solution)/shard_map/mul | solution.py:130
  120.4 3.1 %fusion.93 = f32[4,6,36,128]{3,0,2,1:T(4,128)} fusion(f32[4,6,18,128]{3,0,2,1:T(4,128)S(1)} %get-tuple-element.129, f32[4,6,18,128]{3,0,2,1:T(4,128)S(1)} %get-tuple-element.128, f32[4,14,36,128]{3,0,2,1:T(4,128)S(1)} %subtract_multiply_fusion, s32[]{:T(128)S(6)} %select_n.224, s32[]{:T(128)S(6)} %select_n.223, s32[]{:T(128)S(6)} %select_n.221, ...), kind=kLoop, calls=%fused_computation.192 | loop fusion | flops 2322432 | bytes 2805800 | tf_op jit(solution)/shard_map/mul | solution.py:258
  (75 shorter events, 4.3 us)
Async XLA Ops:
  2.4 0.8 copy-start.3
  5.3 29.4 %collective-permute-start.2 = (f32[4,7,18,128]{3,0,2,1:T(4,128)S(1)}, f32[4,7,18,128]{3,0,2,1:T(4,128)S(1)}, u32[]{:S(2)}, u32[]{:S(2)}) collective-permute-start(f32[4,7,18,128]{3,0,2,1:T(4,128)S(1)} %get-tuple-element.123), channel_id=1, source_target_pairs={{1,0},{2,1},{3,2},{4,3},{5,4},{6,5},{7,6},{8,7},{9,8},{10,9},{11,1... | collective-permute-start | bytes 774152 | tf_op jit(solution)/shard_map/ppermute | solution.py:26
  6.6 28.2 %collective-permute-start.3 = (f32[4,7,18,128]{3,0,2,1:T(4,128)S(1)}, f32[4,7,18,128]{3,0,2,1:T(4,128)S(1)}, u32[]{:S(2)}, u32[]{:S(2)}) collective-permute-start(f32[4,7,18,128]{3,0,2,1:T(4,128)S(1)} %get-tuple-element.123), channel_id=1, source_target_pairs={{2,0},{3,1},{4,2},{5,3},{6,4},{7,5},{8,6},{9,7},{10,8},{11,9},{12,... | collective-permute-start | bytes 774152 | tf_op jit(solution)/shard_map/ppermute | solution.py:26
  7.9 26.9 %collective-permute-start.1 = (f32[4,7,18,128]{3,0,2,1:T(4,128)S(1)}, f32[4,7,18,128]{3,0,2,1:T(4,128)S(1)}, u32[]{:S(2)}, u32[]{:S(2)}) collective-permute-start(f32[4,7,18,128]{3,0,2,1:T(4,128)S(1)} %get-tuple-element.122), channel_id=1, source_target_pairs={{0,2},{1,3},{2,4},{3,5},{4,6},{5,7},{6,8},{7,9},{8,10},{9,11},{10,... | collective-permute-start | bytes 774152 | tf_op jit(solution)/shard_map/ppermute | solution.py:26
  14.4 20.3 %collective-permute-start = (f32[4,7,18,128]{3,0,2,1:T(4,128)S(1)}, f32[4,7,18,128]{3,0,2,1:T(4,128)S(1)}, u32[]{:S(2)}, u32[]{:S(2)}) collective-permute-start(f32[4,7,18,128]{3,0,2,1:T(4,128)S(1)} %get-tuple-element.122), channel_id=1, source_target_pairs={{0,1},{1,2},{2,3},{3,4},{4,5},{5,6},{6,7},{7,8},{8,9},{9,10},{10,1... | collective-permute-start | bytes 774152 | tf_op jit(solution)/shard_map/ppermute | solution.py:26
  42.5 1.2 copy-start.1
  47.5 2.7 %copy-start = (f32[9,6,18,128]{3,0,2,1:T(8,128)}, f32[9,6,18,128]{3,0,2,1:T(8,128)S(1)}, u32[]{:S(2)}) copy-start(f32[9,6,18,128]{3,0,2,1:T(8,128)S(1)} %get-tuple-element.49) | copy-start | bytes 1492996
  47.5 2.6 %copy-start.4 = (f32[4,6,36,128]{3,0,2,1:T(4,128)S(1)}, f32[4,6,36,128]{3,0,2,1:T(4,128)}, u32[]{:S(2)}) copy-start(f32[4,6,36,128]{3,0,2,1:T(4,128)} %copy-done.3) | copy-start | bytes 1327108
  52.7 59.9 %all-to-all-start = ((f32[8,4,7,36,128]{4,1,3,2,0:T(4,128)}), f32[8,4,7,36,128]{4,1,3,2,0:T(4,128)}, u32[]{:S(2)}, u32[]{:S(2)}) async-start(f32[8,4,7,36,128]{4,1,3,2,0:T(4,128)} %stack.2), calls=%async_computation | async-start | bytes 8257536 | tf_op jit(solution)/shard_map/all_to_all | solution.py:201
  69.6 1.0 copy-start.2
  69.6 1.1 copy-start.5
  69.6 1.3 %copy-start.7 = (f32[5,6,18,127]{3,0,2,1:T(8,128)S(1)}, f32[5,6,18,127]{3,0,2,1:T(8,128)}, u32[]{:S(2)}) copy-start(f32[5,6,18,127]{3,0,2,1:T(8,128)} %get-tuple-element.102) | copy-start | bytes 822964
  69.7 1.4 %copy-start.8 = (f32[5,6,18,127]{3,0,2,1:T(8,128)S(1)}, f32[5,6,18,127]{3,0,2,1:T(8,128)}, u32[]{:S(2)}) copy-start(f32[5,6,18,127]{3,0,2,1:T(8,128)} %get-tuple-element.103) | copy-start | bytes 822964
  114.8 1.1 copy-start.9
  114.8 1.1 copy-start.10
  115.9 4.5 %copy-start.6 = (f32[4,6,36,128]{3,0,2,1:T(4,128)S(1)}, f32[4,6,36,128]{3,0,2,1:T(4,128)}, u32[]{:S(2)}) copy-start(f32[4,6,36,128]{3,0,2,1:T(4,128)} %param.13) | copy-start | bytes 1327108
